TPU v7x, 32 devices: a whole 2x2x4 slice. The times are simulated.
32 devices in a mesh: rows: 8 (over z, y), sub: 4 (over x, core).
Axes of the slice: x: 2, y: 2, z: 4, core: 2. Of those that a mesh axis runs over, the one named last changes fastest.
Arguments:
- held: float32 [512, 4, 128, 256], P('rows', 'sub'), may hold values from -256 to 256
- held_block: int32 [512, 4], P('rows', 'sub'), may hold values from 0 to 255, as said below
- held_count: int32 [8, 4], P('rows', 'sub'), may hold values from 0 to 64
Outputs:
- q_factor: float32 [256, 4, 128, 256], P('rows', 'sub')
- r_factor: float32 [256, 256], replicated
Inputs may be any that keep to these rules, and one draw needn't show every extreme that they name: `held_block`: for slots j < held_count of a device, the ids are block numbers of its column group; over all devices of a column group each block is held in exactly one such slot. Slots at or past held_count hold arbitrary ids and data. A device holds at most 8 blocks whose number b has b // 32 equal to any one given device index along rows, and some device reaches that.
All inputs are finite; a program needn't handle non-finite values.
Results may differ from a plain program's by a relative error of at most 0.0003.
Values sent between devices are 32-bit elements; how exact they have to be, the bound alone decides.
No kernel may reach another device: no remote copies, remote signals or barrier semaphores. Data moves between devices by JAX's collectives and lax.ppermute only.
A program may use at most 128 MiB of HBM per device.

v0:
```python
import jax
import jax.numpy as jnp
from jax import lax
from jax.sharding import PartitionSpec as P

BLK_DEV = 32


def factor(gram):
    lower = jnp.linalg.cholesky(gram)
    identity = jnp.eye(gram.shape[0], dtype=gram.dtype)
    inverse = lax.linalg.triangular_solve(lower, identity, left_side=True, lower=True)
    return (lower, inverse)


def gram_of(flattened, total):
    return (
        lax.dot_general(
            flattened,
            flattened,
            (((0,), (0,)), ((), ())),
            precision=lax.Precision.HIGHEST,
            preferred_element_type=jnp.float32,
        )
        / total
    )


def apply_inverse(flattened, inverse):
    return jnp.dot(
        flattened, inverse.T, precision=lax.Precision.HIGHEST, preferred_element_type=jnp.float32
    )


def reduce_gram(partial_value):
    return lax.psum(partial_value, ("rows", "sub"))


def per_device(held, held_block, held_count):
    capacity = held.shape[0]
    block_rows = held.shape[2]
    width = held.shape[3]
    devices_rows = lax.axis_size("rows")
    own_index = lax.axis_index("rows")
    per_slot = max(1, capacity // devices_rows)
    total = float(devices_rows * lax.axis_size("sub") * BLK_DEV * block_rows)
    blocks = held[:, 0]
    block_ids = held_block[:, 0]
    count = held_count[0, 0]
    slots = jnp.arange(capacity, dtype=jnp.int32)
    valid = slots < count
    destination = block_ids // BLK_DEV
    earlier = (
        (destination[:, None] == destination[None, :])
        & valid[None, :]
        & (slots[None, :] < slots[:, None])
    )
    rank_within = jnp.sum(earlier.astype(jnp.int32), axis=1)
    target = jnp.where(valid, destination * per_slot + rank_within, devices_rows * per_slot)
    labels_out = block_ids.astype(jnp.float32)
    outgoing = (
        jnp.zeros((devices_rows * per_slot, block_rows, width), jnp.float32)
        .at[target]
        .set(blocks, mode="drop")
    )
    labels = (
        jnp.full((devices_rows * per_slot,), -1.0, jnp.float32)
        .at[target]
        .set(labels_out, mode="drop")
    )
    arrived = lax.all_to_all(outgoing, "rows", split_axis=0, concat_axis=0, tiled=True)
    arrived_labels = lax.all_to_all(labels, "rows", split_axis=0, concat_axis=0, tiled=True)
    local = arrived_labels.astype(jnp.int32) - own_index * BLK_DEV
    place = jnp.where(arrived_labels >= 0.0, local, BLK_DEV)
    resident = (
        jnp.zeros((BLK_DEV, block_rows, width), jnp.float32).at[place].set(arrived, mode="drop")
    )
    flattened = resident.reshape(-1, width)
    partial_one = gram_of(flattened, total)
    lower_one, inverse_one = factor(reduce_gram(partial_one))
    first = apply_inverse(flattened, inverse_one)
    lower_two, inverse_two = factor(reduce_gram(gram_of(first, total)))
    second, lower_one, lower_two = (apply_inverse(first, inverse_two), lower_one, lower_two)
    result = second.reshape(BLK_DEV, block_rows, width)
    r_factor = jnp.dot(
        lower_two.T,
        lower_one.T,
        precision=lax.Precision.HIGHEST,
        preferred_element_type=jnp.float32,
    )
    return (result[:, None], r_factor)


def solution(mesh):
    in_specs = (P("rows", "sub", None, None), P("rows", "sub"), P("rows", "sub"))
    out_specs = (P("rows", "sub", None, None), P())
    return jax.shard_map(
        per_device, mesh=mesh, in_specs=in_specs, out_specs=out_specs, check_vma=False
    )
```

profile of v0, /device:TPU:0, one launch (start us, length us, event | category | flops | bytes accessed | tf_op | source)
XLA Modules:
  0.0 661.5 jit_solution(13611043332102278474)
XLA Ops:
  7.2 0.7 bitcast_convert_fusion
  7.8 0.7 and_select_fusion
  9.2 0.2 convert_reduce_fusion
  9.3 0.8 scatter_custom_fusion
  10.1 0.7 all_to_all.9
  10.8 7.3 %all-to-all-start = ((f32[8,8,1]{1,2,0:T(1,128)}), f32[8,8,1]{1,2,0:T(1,128)S(1)}, u32[]{:S(2)}, u32[]{:S(2)}) async-start(f32[8,8,1]{1,2,0:T(1,128)} %bitcast.5), calls=%async_computation | async-start | bytes 8192 | tf_op jit(solution)/shard_map/all_to_all | solution.py:72
  18.1 4.2 broadcast_in_dim.26
  22.3 16.0 %scatter_fusion = f32[64,128,256]{2,1,0:T(8,128)} fusion(f32[64,128,256]{2,1,0:T(8,128)} %broadcast_in_dim.26, s32[64]{0:T(128)S(1)} %fusion.38, f32[64,128,256]{2,1,0:T(8,128)} %bitcast.102), kind=kCustom, calls=%fused_computation.1 | custom fusion | bytes 25166080 | tf_op jit(solution)/shard_map/scatter | solution.py:64
  38.4 0.0 all-to-all-done
  38.4 5.8 all-to-all-start.1
  44.2 0.0 all-reduce.4.cloned.1.call-start
  44.3 0.1 select_n.54
  44.4 182.5 %all-to-all-done.1 = f32[64,128,256]{2,1,0:T(8,128)} async-done(((f32[64,128,256]{2,1,0:T(8,128)}), f32[64,128,256]{2,1,0:T(8,128)}, u32[]{:S(2)}, u32[]{:S(2)}) %all-to-all-start.1) | async-done | bytes 8388640 | tf_op jit(solution)/shard_map/all_to_all | solution.py:71
  226.9 2.5 broadcast_in_dim.11
  229.4 15.4 %scatter_fusion.1 = f32[32,128,256]{2,1,0:T(8,128)} fusion(f32[32,128,256]{2,1,0:T(8,128)} %broadcast_in_dim.11, s32[64]{0:T(128)S(1)} %fusion.37, f32[64,128,256]{2,1,0:T(8,128)} %all-to-all-done.1), kind=kCustom, calls=%fused_computation.2 | custom fusion | bytes 25166080 | tf_op jit(solution)/shard_map/scatter | solution.py:76
  244.8 10.9 %fusion = f32[256,256]{0,1:T(8,128)} fusion(f32[32,128,256]{2,1,0:T(8,128)} %scatter_fusion.1), kind=kOutput, calls=%fused_computation.9 | convolution fusion | flops 3221291008 | bytes 4456448 | tf_op jit(solution)/shard_map/dot_general | solution.py:18
  255.7 0.0 all-reduce.4.cloned.1.call-update
  255.7 0.2 all-reduce.6.cloned.1.call-start
  256.0 124.2 %all-reduce.4.cloned.1.call-done = f32[256,256]{0,1:T(8,128)} async-done(((f32[256,256]{0,1:T(8,128)}), f32[256,256]{0,1:T(8,128)}) %all-reduce.4.cloned.1.call-update) | async-done | bytes 262160 | tf_op jit(solution)/shard_map/psum | solution.py:36
  380.2 1.1 copy.27
  381.3 1.0 fusion.10
  382.3 11.7 %cholesky.130 = f32[128,128]{1,0:T(8,128)S(1)} custom-call(f32[128,128]{1,0:T(8,128)S(1)} %cholesky.194), custom_call_target="Cholesky" | custom-call | tf_op jit(solution)/shard_map/jit(cholesky)/cholesky | solution.py:10
  394.0 9.8 %custom-call.13 = f32[1,128,128]{1,2,0:T(8,128)S(1)} custom-call(f32[1,128,128]{2,1,0:T(8,128)S(1)} %get-tuple-element.55), custom_call_target="InvertDiagBlocksLowerTriangular" | custom-call | tf_op jit(solution)/shard_map/jit(cholesky)/cholesky | solution.py:10
  403.9 0.2 constant_dynamic-update-slice_fusion.3
  404.1 0.3 convolution_subtract_fusion.3
  404.4 11.7 %cholesky.147 = f32[128,128]{1,0:T(8,128)S(1)} custom-call(f32[128,128]{1,0:T(8,128)S(1)} %convolution_subtract_fusion.3), custom_call_target="Cholesky" | custom-call | tf_op jit(solution)/shard_map/jit(cholesky)/cholesky | solution.py:10
  416.1 0.7 compare_reduce_fusion.2
  418.2 0.1 broadcast.203
  418.3 4.1 while.4
  418.3 0.6 fusion.63
  418.9 1.4 bitcast_dynamic-update-slice_fusion.4
  420.4 0.6 fusion.63
  421.0 1.4 bitcast_dynamic-update-slice_fusion.4
  422.4 19.7 %custom-call.14 = f32[2,128,128]{1,2,0:T(8,128)S(1)} custom-call(f32[2,128,128]{2,1,0:T(8,128)S(1)} %get-tuple-element.18), custom_call_target="InvertDiagBlocksLowerTriangular" | custom-call | tf_op jit(solution)/shard_map/triangular_solve/custom-call.0 | solution.py:12
  442.1 0.3 fusion.23
  442.4 0.3 convolution_subtract_fusion.1
  442.7 0.3 fusion.30
  443.0 5.5 fusion.1
  448.5 0.0 copy-start
  448.5 1.9 copy-done
  450.4 7.4 %convolution_multiply_fusion = f32[256,256]{0,1:T(8,128)} fusion(f32[4096,256]{1,0:T(8,128)S(1)} %fusion.1), kind=kOutput, calls=%fused_computation.7 | convolution fusion | flops 3221291008 | bytes 4456448 | tf_op jit(solution)/shard_map/dot_general | solution.py:18
  457.9 0.0 all-reduce.6.cloned.1.call-update
  457.9 124.1 %all-reduce.6.cloned.1.call-done = f32[256,256]{0,1:T(8,128)} async-done(((f32[256,256]{0,1:T(8,128)}), f32[256,256]{0,1:T(8,128)}) %all-reduce.6.cloned.1.call-update) | async-done | bytes 262160 | tf_op jit(solution)/shard_map/psum | solution.py:36
  582.0 1.1 copy.29
  583.1 1.0 fusion.9
  584.1 11.7 %cholesky.164 = f32[128,128]{1,0:T(8,128)S(1)} custom-call(f32[128,128]{1,0:T(8,128)S(1)} %cholesky.197), custom_call_target="Cholesky" | custom-call | tf_op jit(solution)/shard_map/jit(cholesky)/cholesky | solution.py:10
  595.9 10.2 %custom-call.15 = f32[1,128,128]{1,2,0:T(8,128)S(1)} custom-call(f32[1,128,128]{2,1,0:T(8,128)S(1)} %get-tuple-element.51), custom_call_target="InvertDiagBlocksLowerTriangular" | custom-call | tf_op jit(solution)/shard_map/jit(cholesky)/cholesky | solution.py:10
  606.1 0.2 constant_dynamic-update-slice_fusion.1
  606.3 0.3 convolution_subtract_fusion.2
  606.6 11.7 %cholesky.181 = f32[128,128]{1,0:T(8,128)S(1)} custom-call(f32[128,128]{1,0:T(8,128)S(1)} %convolution_subtract_fusion.2), custom_call_target="Cholesky" | custom-call | tf_op jit(solution)/shard_map/jit(cholesky)/cholesky | solution.py:10
  618.3 0.6 compare_reduce_fusion
  619.0 0.6 compare_reduce_fusion.1
  620.9 1.2 fusion.15
  622.1 3.9 while.5
  622.2 0.6 fusion.64
  622.7 1.4 bitcast_dynamic-update-slice_fusion.5
  624.1 0.6 fusion.64
  624.7 1.4 bitcast_dynamic-update-slice_fusion.5
  626.1 19.8 %custom-call.16 = f32[2,128,128]{1,2,0:T(8,128)S(1)} custom-call(f32[2,128,128]{2,1,0:T(8,128)S(1)} %get-tuple-element.19), custom_call_target="InvertDiagBlocksLowerTriangular" | custom-call | tf_op jit(solution)/shard_map/triangular_solve/custom-call.0 | solution.py:12
  645.9 0.3 fusion.21
  646.3 0.3 convolution_subtract_fusion
  646.5 0.3 fusion.26
  646.8 7.7 %fusion.5 = f32[4096,256]{1,0:T(8,128)} fusion(f32[4096,256]{1,0:T(8,128)} %copy-done, f32[128,256]{1,0:T(8,128)S(1)} %fusion.26, f32[128,256]{1,0:T(8,128)S(1)} %fusion.21), kind=kOutput, calls=%fused_computation.18 | convolution fusion | flops 3221291008 | bytes 8650752 | tf_op jit(solution)/shard_map/dot_general | solution.py:30
  (22 shorter events, 0.4 us)
Async XLA Ops:
  10.8 27.6 %all-to-all-start = ((f32[8,8,1]{1,2,0:T(1,128)}), f32[8,8,1]{1,2,0:T(1,128)S(1)}, u32[]{:S(2)}, u32[]{:S(2)}) async-start(f32[8,8,1]{1,2,0:T(1,128)} %bitcast.5), calls=%async_computation | async-start | bytes 8192 | tf_op jit(solution)/shard_map/all_to_all | solution.py:72
  38.4 188.5 %all-to-all-start.1 = ((f32[64,128,256]{2,1,0:T(8,128)}), f32[64,128,256]{2,1,0:T(8,128)}, u32[]{:S(2)}, u32[]{:S(2)}) async-start(f32[64,128,256]{2,1,0:T(8,128)} %scatter_fusion), calls=%async_computation.1 | async-start | bytes 16777216 | tf_op jit(solution)/shard_map/all_to_all | solution.py:71
  44.2 335.9 %all-reduce.4.cloned.1.call-start = ((), (), s32[]{:S(2)}) async-start(), calls=%async_computation.2 | async-start | bytes 524288 | tf_op jit(solution)/shard_map/psum | solution.py:36
  255.7 326.3 %all-reduce.6.cloned.1.call-start = ((), (), s32[]{:S(2)}) async-start(), calls=%async_computation.3 | async-start | bytes 524288 | tf_op jit(solution)/shard_map/psum | solution.py:36
  448.5 1.9 copy-start
Sparse Core Ops, SparseCore 0:
  255.8 124.3 all-reduce.3
  458.0 123.9 all-reduce.5
where the time goes:
time: 669 us; the launch traced here: 662 us
  waiting for transfers between devices  431 us (64%)
  other arithmetic  112 us (17%)
  local copies, waits for them, and re-layouts  51.9 us (8%)
  matrix products  35.4 us (5%)
  between operations  17.8 us (3%)
  starting transfers between devices  13.4 us (2%)
    psum x2, waiting for transfers between devices, reduce_gram(): return lax.psum(partial_value, ('rows', 'sub'))  248 us
    all_to_all x1, waiting for transfers between devices, per_device(): lax.all_to_all(outgoing, 'rows', split_axis=0, concat_axis=0, tiled=True)  182 us
    another operation x13, other arithmetic, factor(): lower = jnp.linalg.cholesky(gram)  69 us
    another operation x5, other arithmetic, factor(): lax.linalg.triangular_solve(lower, identity, left_side=True, lower=True)  39.6 us
    dot_general x2, matrix products, gram_of(): lax.dot_general(flattened, flattened, (((0,), (0,)), ((), ())), precision...  18.3 us
    scatter x1, local copies, waits for them, and re-layouts, per_device(): outgoing = jnp.zeros((devices_rows * per_slot, block_rows, width), jnp.fl...  16 us
    scatter x1, local copies, waits for them, and re-layouts, per_device(): jnp.zeros((BLK_DEV, block_rows, width), jnp.float32).at[place]  15.4 us
  transfers between devices with their start and end apart: 4, of which 3 were waited for; matrix products, arithmetic and copies ran while one was open for 3% of the time, Pallas kernels for 0%

commit v1 on v0

--- a/solution.py
+++ b/solution.py
@@ -4,6 +4,11 @@
 from jax.sharding import PartitionSpec as P
 
 BLK_DEV = 32
+
+
+def check_tracks(piece_in):
+    back = jax.lax.psum(jax.lax.psum(piece_in, "sub"), "rows")
+    return back
 
 
 def factor(gram):
@@ -33,7 +38,7 @@
 
 
 def reduce_gram(partial_value):
-    return lax.psum(partial_value, ("rows", "sub"))
+    return check_tracks(partial_value)
 
 
 def per_device(held, held_block, held_count):

time: 669 us -> 631 us (0.943)
  waiting for transfers between devices: 431 us -> 393 us
    psum x2 -> x4, waiting for transfers between devices: 248 us -> 210 us  [check_tracks(): back = jax.lax.psum(jax.lax.psum(piece_in, 'sub'), 'rows')]
  transfers between devices with their start and end apart: 4 -> 6, of which waited for: 3 -> 5; matrix products, arithmetic and copies ran while one was open for 3% -> 3% of each run, Pallas kernels for 0% -> 0%
where the time goes in v1:
time: 631 us; the launch traced here: 623 us
  waiting for transfers between devices  393 us (62%)
  other arithmetic  112 us (18%)
  local copies, waits for them, and re-layouts  51.9 us (8%)
  matrix products  35.2 us (6%)
  between operations  17.4 us (3%)
  starting transfers between devices  13.9 us (2%)
    psum x4, waiting for transfers between devices, check_tracks(): back = jax.lax.psum(jax.lax.psum(piece_in, 'sub'), 'rows')  210 us
    all_to_all x1, waiting for transfers between devices, per_device(): lax.all_to_all(outgoing, 'rows', split_axis=0, concat_axis=0, tiled=True)  182 us
    another operation x13, other arithmetic, factor(): lower = jnp.linalg.cholesky(gram)  68.6 us
    another operation x5, other arithmetic, factor(): lax.linalg.triangular_solve(lower, identity, left_side=True, lower=True)  39.4 us
    dot_general x2, matrix products, gram_of(): lax.dot_general(flattened, flattened, (((0,), (0,)), ((), ())), precision...  18.3 us
    scatter x1, local copies, waits for them, and re-layouts, per_device(): outgoing = jnp.zeros((devices_rows * per_slot, block_rows, width), jnp.fl...  16 us
    scatter x1, local copies, waits for them, and re-layouts, per_device(): jnp.zeros((BLK_DEV, block_rows, width), jnp.float32).at[place]  15.4 us
    dot_general x2, matrix products, apply_inverse(): jnp.dot(flattened, inverse.T, precision=lax.Precision.HIGHEST, preferred_...  13 us
  transfers between devices with their start and end apart: 6, of which 5 were waited for; matrix products, arithmetic and copies ran while one was open for 3% of the time, Pallas kernels for 0%

profile of v1, /device:TPU:0, one launch (start us, length us, event | category | flops | bytes accessed | tf_op | source)
XLA Modules:
  0.0 623.3 jit_solution(18007971331506997065)
XLA Ops:
  7.2 0.7 bitcast_convert_fusion
  7.8 0.7 and_select_fusion
  9.2 0.2 convert_reduce_fusion
  9.3 0.8 scatter_custom_fusion
  10.1 0.7 all_to_all.9
  10.8 7.3 %all-to-all-start = ((f32[8,8,1]{1,2,0:T(1,128)}), f32[8,8,1]{1,2,0:T(1,128)S(1)}, u32[]{:S(2)}, u32[]{:S(2)}) async-start(f32[8,8,1]{1,2,0:T(1,128)} %bitcast.5), calls=%async_computation | async-start | bytes 8192 | tf_op jit(solution)/shard_map/all_to_all | solution.py:77
  18.1 4.2 broadcast_in_dim.26
  22.3 16.0 %scatter_fusion = f32[64,128,256]{2,1,0:T(8,128)} fusion(f32[64,128,256]{2,1,0:T(8,128)} %broadcast_in_dim.26, s32[64]{0:T(128)S(1)} %fusion.38, f32[64,128,256]{2,1,0:T(8,128)} %bitcast.102), kind=kCustom, calls=%fused_computation.1 | custom fusion | bytes 25166080 | tf_op jit(solution)/shard_map/scatter | solution.py:69
  38.4 5.8 all-to-all-start.1
  44.2 0.0 all-reduce.6.cloned.1.call-start
  44.3 0.1 select_n.54
  44.4 182.5 %all-to-all-done.1 = f32[64,128,256]{2,1,0:T(8,128)} async-done(((f32[64,128,256]{2,1,0:T(8,128)}), f32[64,128,256]{2,1,0:T(8,128)}, u32[]{:S(2)}, u32[]{:S(2)}) %all-to-all-start.1) | async-done | bytes 8388640 | tf_op jit(solution)/shard_map/all_to_all | solution.py:76
  226.9 2.5 broadcast_in_dim.11
  229.4 15.4 %scatter_fusion.1 = f32[32,128,256]{2,1,0:T(8,128)} fusion(f32[32,128,256]{2,1,0:T(8,128)} %broadcast_in_dim.11, s32[64]{0:T(128)S(1)} %fusion.37, f32[64,128,256]{2,1,0:T(8,128)} %all-to-all-done.1), kind=kCustom, calls=%fused_computation.2 | custom fusion | bytes 25166080 | tf_op jit(solution)/shard_map/scatter | solution.py:81
  244.8 10.9 %fusion = f32[256,256]{0,1:T(8,128)} fusion(f32[32,128,256]{2,1,0:T(8,128)} %scatter_fusion.1), kind=kOutput, calls=%fused_computation.9 | convolution fusion | flops 3221291008 | bytes 4456448 | tf_op jit(solution)/shard_map/dot_general | solution.py:23
  255.7 0.0 all-reduce.6.cloned.1.call-update
  255.7 0.0 all-reduce.8.cloned.1.call-start
  255.8 31.4 %all-reduce.6.cloned.1.call-done = f32[256,256]{0,1:T(8,128)} async-done(((f32[256,256]{0,1:T(8,128)}), f32[256,256]{0,1:T(8,128)}) %all-reduce.6.cloned.1.call-update) | async-done | bytes 262160 | tf_op jit(solution)/shard_map/psum | solution.py:10
  287.1 0.2 all-reduce.10.cloned.1.call-start
  287.4 74.0 %all-reduce.8.cloned.1.call-done = f32[256,256]{0,1:T(8,128)} async-done(((f32[256,256]{0,1:T(8,128)}), f32[256,256]{0,1:T(8,128)}) %all-reduce.8.cloned.1.call-update) | async-done | bytes 262160 | tf_op jit(solution)/shard_map/psum | solution.py:10
  361.4 1.1 copy.27
  362.5 1.0 fusion.10
  363.5 11.7 %cholesky.130 = f32[128,128]{1,0:T(8,128)S(1)} custom-call(f32[128,128]{1,0:T(8,128)S(1)} %cholesky.194), custom_call_target="Cholesky" | custom-call | tf_op jit(solution)/shard_map/jit(cholesky)/cholesky | solution.py:15
  375.2 9.8 %custom-call.13 = f32[1,128,128]{1,2,0:T(8,128)S(1)} custom-call(f32[1,128,128]{2,1,0:T(8,128)S(1)} %get-tuple-element.55), custom_call_target="InvertDiagBlocksLowerTriangular" | custom-call | tf_op jit(solution)/shard_map/jit(cholesky)/cholesky | solution.py:15
  385.1 0.2 constant_dynamic-update-slice_fusion.3
  385.3 0.3 convolution_subtract_fusion.3
  385.6 11.7 %cholesky.147 = f32[128,128]{1,0:T(8,128)S(1)} custom-call(f32[128,128]{1,0:T(8,128)S(1)} %convolution_subtract_fusion.3), custom_call_target="Cholesky" | custom-call | tf_op jit(solution)/shard_map/jit(cholesky)/cholesky | solution.py:15
  397.3 0.7 compare_reduce_fusion.2
  399.3 0.1 broadcast.203
  399.4 4.3 while.4
  399.7 0.7 fusion.63
  400.3 1.3 bitcast_dynamic-update-slice_fusion.4
  401.7 0.7 fusion.63
  402.4 1.3 bitcast_dynamic-update-slice_fusion.4
  403.7 19.7 %custom-call.14 = f32[2,128,128]{1,2,0:T(8,128)S(1)} custom-call(f32[2,128,128]{2,1,0:T(8,128)S(1)} %get-tuple-element.18), custom_call_target="InvertDiagBlocksLowerTriangular" | custom-call | tf_op jit(solution)/shard_map/triangular_solve/custom-call.0 | solution.py:17
  423.4 0.3 fusion.23
  423.7 0.3 convolution_subtract_fusion.1
  424.0 0.3 fusion.30
  424.3 5.3 fusion.1
  429.6 1.9 copy-done
  431.5 7.4 %convolution_multiply_fusion = f32[256,256]{0,1:T(8,128)} fusion(f32[4096,256]{1,0:T(8,128)S(1)} %fusion.1), kind=kOutput, calls=%fused_computation.7 | convolution fusion | flops 3221291008 | bytes 4456448 | tf_op jit(solution)/shard_map/dot_general | solution.py:23
  439.0 0.4 all-reduce.12.cloned.1.call-start
  439.4 30.9 %all-reduce.10.cloned.1.call-done = f32[256,256]{0,1:T(8,128)} async-done(((f32[256,256]{0,1:T(8,128)}), f32[256,256]{0,1:T(8,128)}) %all-reduce.10.cloned.1.call-update) | async-done | bytes 262160 | tf_op jit(solution)/shard_map/psum | solution.py:10
  470.4 74.1 %all-reduce.12.cloned.1.call-done = f32[256,256]{0,1:T(8,128)} async-done(((f32[256,256]{0,1:T(8,128)}), f32[256,256]{0,1:T(8,128)}) %all-reduce.12.cloned.1.call-update) | async-done | bytes 262160 | tf_op jit(solution)/shard_map/psum | solution.py:10
  544.5 1.1 copy.29
  545.6 1.0 fusion.9
  546.6 11.7 %cholesky.164 = f32[128,128]{1,0:T(8,128)S(1)} custom-call(f32[128,128]{1,0:T(8,128)S(1)} %cholesky.197), custom_call_target="Cholesky" | custom-call | tf_op jit(solution)/shard_map/jit(cholesky)/cholesky | solution.py:15
  558.4 9.8 %custom-call.15 = f32[1,128,128]{1,2,0:T(8,128)S(1)} custom-call(f32[1,128,128]{2,1,0:T(8,128)S(1)} %get-tuple-element.51), custom_call_target="InvertDiagBlocksLowerTriangular" | custom-call | tf_op jit(solution)/shard_map/jit(cholesky)/cholesky | solution.py:15
  568.2 0.2 constant_dynamic-update-slice_fusion.1
  568.4 0.3 convolution_subtract_fusion.2
  568.7 11.7 %cholesky.181 = f32[128,128]{1,0:T(8,128)S(1)} custom-call(f32[128,128]{1,0:T(8,128)S(1)} %convolution_subtract_fusion.2), custom_call_target="Cholesky" | custom-call | tf_op jit(solution)/shard_map/jit(cholesky)/cholesky | solution.py:15
  580.4 0.6 compare_reduce_fusion
  581.1 0.6 compare_reduce_fusion.1
  583.0 1.2 fusion.15
  584.2 4.1 while.5
  584.4 0.6 fusion.64
  585.0 1.4 bitcast_dynamic-update-slice_fusion.5
  586.4 0.6 fusion.64
  587.0 1.4 bitcast_dynamic-update-slice_fusion.5
  588.4 19.7 %custom-call.16 = f32[2,128,128]{1,2,0:T(8,128)S(1)} custom-call(f32[2,128,128]{2,1,0:T(8,128)S(1)} %get-tuple-element.19), custom_call_target="InvertDiagBlocksLowerTriangular" | custom-call | tf_op jit(solution)/shard_map/triangular_solve/custom-call.0 | solution.py:17
  608.1 0.3 fusion.21
  608.4 0.3 convolution_subtract_fusion
  608.6 0.3 fusion.26
  609.0 7.7 %fusion.5 = f32[4096,256]{1,0:T(8,128)} fusion(f32[4096,256]{1,0:T(8,128)} %copy-done, f32[128,256]{1,0:T(8,128)S(1)} %fusion.26, f32[128,256]{1,0:T(8,128)S(1)} %fusion.21), kind=kOutput, calls=%fused_computation.18 | convolution fusion | flops 3221291008 | bytes 8650752 | tf_op jit(solution)/shard_map/dot_general | solution.py:35
  (27 shorter events, 0.4 us)
Async XLA Ops:
  10.8 27.6 %all-to-all-start = ((f32[8,8,1]{1,2,0:T(1,128)}), f32[8,8,1]{1,2,0:T(1,128)S(1)}, u32[]{:S(2)}, u32[]{:S(2)}) async-start(f32[8,8,1]{1,2,0:T(1,128)} %bitcast.5), calls=%async_computation | async-start | bytes 8192 | tf_op jit(solution)/shard_map/all_to_all | solution.py:77
  38.4 188.5 %all-to-all-start.1 = ((f32[64,128,256]{2,1,0:T(8,128)}), f32[64,128,256]{2,1,0:T(8,128)}, u32[]{:S(2)}, u32[]{:S(2)}) async-start(f32[64,128,256]{2,1,0:T(8,128)} %scatter_fusion), calls=%async_computation.1 | async-start | bytes 16777216 | tf_op jit(solution)/shard_map/all_to_all | solution.py:76
  44.2 242.9 %all-reduce.6.cloned.1.call-start = ((), (), s32[]{:S(2)}) async-start(), calls=%async_computation.2 | async-start | bytes 524288 | tf_op jit(solution)/shard_map/psum | solution.py:10
  255.7 105.7 %all-reduce.8.cloned.1.call-start = ((), (), s32[]{:S(2)}) async-start(), calls=%async_computation.3 | async-start | bytes 524288 | tf_op jit(solution)/shard_map/psum | solution.py:10
  287.1 183.2 %all-reduce.10.cloned.1.call-start = ((), (), s32[]{:S(2)}) async-start(), calls=%async_computation.4 | async-start | bytes 524288 | tf_op jit(solution)/shard_map/psum | solution.py:10
  429.6 1.9 copy-start
  439.0 105.5 %all-reduce.12.cloned.1.call-start = ((), (), s32[]{:S(2)}) async-start(), calls=%async_computation.5 | async-start | bytes 524288 | tf_op jit(solution)/shard_map/psum | solution.py:10
Sparse Core Ops, SparseCore 0:
  255.8 31.2 all-reduce.5
  290.8 70.5 all-reduce.7
  439.1 31.2 all-reduce.9
  473.9 70.5 all-reduce.11
